TPU v7x, 256 devices: a whole 4x4x8 slice. The times are simulated.
256 devices in a mesh: ctx: 16 (over z_lo, y), dp: 16 (over x, z_hi, core).
Axes of the slice: x: 4, y: 4, z: 8 (z_hi: 2, z_lo: 4; z = z_hi * 4 + z_lo), core: 2. Of those that a mesh axis runs over, the one named last changes fastest.
Arguments:
- inputs: bfloat16 [16, 2048, 4096], P('dp', 'ctx'), may hold values from -6 to 6
- b_proj: bfloat16 [16, 2048, 512], P('dp', 'ctx'), may hold values from -0.75 to 0.75
- c_proj: bfloat16 [16, 2048, 512], P('dp', 'ctx'), may hold values from -0.75 to 0.75
- dt_raw: float32 [16, 64, 2048], P('dp', None, 'ctx'), may hold values from -3 to 9
- a_log: float32 [64], P('dp'), may hold values from -12 to -3
- dt_bias: float32 [64], P('dp'), may hold values from 0.2 to 0.8
- d_skip: float32 [64], P('dp'), may hold values from 0.5 to 1.5
- grad_out: bfloat16 [16, 2048, 4096], P('dp', 'ctx'), may hold values from -6 to 6
Outputs:
- grad_inputs: bfloat16 [16, 2048, 4096], P('dp', 'ctx')
- grad_b: bfloat16 [16, 2048, 512], P('dp', 'ctx')
- grad_c: bfloat16 [16, 2048, 512], P('dp', 'ctx')
- grad_dt: float32 [16, 64, 2048], P('dp', None, 'ctx')
- grad_alog: float32 [64], P('dp')
- grad_bias: float32 [64], P('dp')
- grad_skip: float32 [64], P('dp')
All inputs are finite; a program needn't handle non-finite values.
Results may differ from a plain program's by a relative error of at most 0.0014.
Values sent between devices are 32-bit elements; how exact they have to be, the bound alone decides.
No kernel may reach another device: no remote copies, remote signals or barrier semaphores. Data moves between devices by JAX's collectives and lax.ppermute only.
A program may use at most 192 MiB of HBM per device.

v0:
```python
import jax
import jax.numpy as jnp
from jax import lax
from jax.sharding import PartitionSpec as P

P_SIZE = 64
N = 64
G = 8
SPAN = 128


highest = lax.Precision.HIGHEST


def carried_in(part, axis, combine, identity, reverse):
    count = lax.axis_size(axis)
    place = lax.axis_index(axis)
    ahead = count - 1 - place if reverse else place
    gathered = jax.tree.map(lambda a: lax.all_gather(a, axis), part)
    state = jax.tree.map(lambda a, e: jnp.zeros_like(a) + jnp.asarray(e, a.dtype), part, identity)

    def one(hop, state):
        source = count - 1 - hop if reverse else hop
        return combine(
            state, jax.tree.map(lambda a: lax.dynamic_index_in_dim(a, source, 0, False), gathered)
        )

    return lax.fori_loop(0, ahead, one, state)


def group_scan(group_in, b_group, c_group, raw_group, bias_group, alog_group, skip_group, state_in):
    length, num_heads, head_width = group_in.shape
    blocks = length // SPAN
    dt_value = jax.nn.softplus(raw_group + bias_group[:, None])
    log_decay = dt_value * (-jnp.exp(alog_group))[:, None]
    cumulative = jnp.cumsum(log_decay.reshape(num_heads, blocks, SPAN), axis=2)
    scaled = (group_in * dt_value.T[:, :, None]).reshape(blocks, SPAN, num_heads, head_width)
    b_blocks = b_group.reshape(blocks, SPAN, N)
    c_blocks = c_group.reshape(blocks, SPAN, N)
    scores = jnp.einsum("cqn,ckn->cqk", c_blocks, b_blocks, precision=highest)
    offsets = jnp.arange(SPAN)
    causal = offsets[:, None] >= offsets[None, :]
    spread = cumulative[:, :, :, None] - cumulative[:, :, None, :]
    weights = jnp.where(causal, jnp.exp(jnp.where(causal, spread, 0.0)), 0.0)
    local_part = jnp.einsum("hcqk,ckhp->cqhp", weights * scores[None], scaled, precision=highest)
    tail_decay = jnp.exp(cumulative[:, :, -1:] - cumulative)
    weighted_b = b_blocks[None] * tail_decay[:, :, :, None]
    block_states = jnp.einsum("hckn,ckhp->chpn", weighted_b, scaled, precision=highest)
    block_decay = jnp.exp(cumulative[:, :, -1]).T

    def advance(running, block_item):
        factor, newest = block_item
        return (factor[:, None, None] * running + newest, running)

    state_out, entering = lax.scan(advance, state_in, (block_decay, block_states))
    cross_part = jnp.einsum("cqn,chpn->cqhp", c_blocks, entering, precision=highest)
    cross_part = cross_part * jnp.exp(cumulative).transpose(1, 2, 0)[:, :, :, None]
    result = (local_part + cross_part).reshape(length, num_heads, head_width)
    result = result + skip_group[None, :, None] * group_in
    return (result, state_out)


def group_grads(
    group_in,
    b_group,
    c_group,
    raw_group,
    bias_group,
    alog_group,
    skip_group,
    grad_group,
    state_in,
    state_grad,
):
    primal, pullback = jax.vjp(
        group_scan,
        group_in,
        b_group,
        c_group,
        raw_group,
        bias_group,
        alog_group,
        skip_group,
        state_in,
    )
    return pullback((grad_group, state_grad))


def slab_terms(pieces):
    group_in, b_group, c_group, raw_group, bias_group, alog_group, skip_group, grad_group = pieces
    dt_value = jax.nn.softplus(raw_group + bias_group[:, None])
    log_decay = dt_value * (-jnp.exp(alog_group))[:, None]
    cumulative = jnp.cumsum(log_decay, axis=1)
    total = cumulative[:, -1]
    tail_decay = jnp.exp(total[:, None] - cumulative)
    carried = group_in * (dt_value * tail_decay).T[:, :, None]
    local_state = jnp.einsum("tn,thp->hpn", b_group, carried, precision=highest)
    weighted_grad = grad_group * jnp.exp(cumulative).T[:, :, None]
    local_source = jnp.einsum("tn,thp->hpn", c_group, weighted_grad, precision=highest)
    return (jnp.exp(total), local_state, local_source)


def chain_pair(earlier, later):
    return (earlier[0] * later[0], later[0][:, None, None] * earlier[1] + later[1])


def run_backward(pieces, state_in, state_grad):
    group_in, b_group, c_group, raw_group, bias_group, alog_group, skip_group, grad_group = pieces
    return group_grads(
        group_in,
        b_group,
        c_group,
        raw_group,
        bias_group,
        alog_group,
        skip_group,
        grad_group,
        state_in,
        state_grad,
    )


def per_device(inputs, b_proj, c_proj, dt_raw, a_log, dt_bias, d_skip, grad_out):
    a_log, dt_bias, d_skip = (
        lax.all_gather(a_log, "dp", axis=0, tiled=True),
        lax.all_gather(dt_bias, "dp", axis=0, tiled=True),
        lax.all_gather(d_skip, "dp", axis=0, tiled=True),
    )
    tokens = inputs.shape[1]
    num_heads = a_log.shape[0]
    group_heads = num_heads // G
    head_in = inputs[0].reshape(tokens, G, group_heads, P_SIZE)
    head_grad = grad_out[0].reshape(tokens, G, group_heads, P_SIZE)
    b_all = b_proj[0].reshape(tokens, G, N)
    c_all = c_proj[0].reshape(tokens, G, N)
    raw_all = dt_raw[0].reshape(G, group_heads, tokens)
    bias_all = dt_bias.reshape(G, group_heads)
    alog_all = a_log.reshape(G, group_heads)
    skip_all = d_skip.reshape(G, group_heads)
    sliced = []
    for group in range(G):
        sliced.append(
            (
                head_in[:, group].astype(jnp.float32),
                b_all[:, group].astype(jnp.float32),
                c_all[:, group].astype(jnp.float32),
                raw_all[group],
                bias_all[group],
                alog_all[group],
                skip_all[group],
                head_grad[:, group].astype(jnp.float32),
            )
        )
    collected = []
    factors, states, sources = ([], [], [])
    for group in range(G):
        factor, local_state, local_source = slab_terms(sliced[group])
        factors.append(factor)
        states.append(local_state)
        sources.append(local_source)
    factor_all = jnp.concatenate(factors, axis=0)
    state_all = jnp.concatenate(states, axis=0)
    source_all = jnp.concatenate(sources, axis=0)
    identity = (jnp.ones_like(factor_all), jnp.zeros_like(state_all))
    entering = carried_in((factor_all, state_all), "ctx", chain_pair, identity, False)[1]
    leaving = carried_in((factor_all, source_all), "ctx", chain_pair, identity, True)[1]
    for group in range(G):
        window = slice(group * group_heads, (group + 1) * group_heads)
        collected.append(run_backward(sliced[group], entering[window], leaving[window]))
    grad_inputs = (
        jnp.concatenate([entry[0] for entry in collected], axis=1)
        .reshape(tokens, num_heads * P_SIZE)
        .astype(jnp.bfloat16)[None]
    )
    grad_b = (
        jnp.stack([entry[1] for entry in collected], axis=1)
        .reshape(tokens, G * N)
        .astype(jnp.bfloat16)[None]
    )
    grad_c = (
        jnp.stack([entry[2] for entry in collected], axis=1)
        .reshape(tokens, G * N)
        .astype(jnp.bfloat16)[None]
    )
    grad_dt = jnp.concatenate([entry[3] for entry in collected], axis=0)[None]
    head_stats = jnp.stack(
        [
            jnp.concatenate([entry[5] for entry in collected]),
            jnp.concatenate([entry[4] for entry in collected]),
            jnp.concatenate([entry[6] for entry in collected]),
        ],
        axis=0,
    )
    share_size = num_heads // lax.axis_size("dp")
    summed = lax.psum(head_stats, ("ctx", "dp"))
    own_totals = lax.dynamic_slice_in_dim(summed, lax.axis_index("dp") * share_size, share_size, 1)
    return (grad_inputs, grad_b, grad_c, grad_dt, own_totals[0], own_totals[1], own_totals[2])


def solution(mesh):
    in_specs = (
        P("dp", "ctx", None),
        P("dp", "ctx", None),
        P("dp", "ctx", None),
        P("dp", None, "ctx"),
        P("dp"),
        P("dp"),
        P("dp"),
        P("dp", "ctx", None),
    )
    out_specs = (
        P("dp", "ctx", None),
        P("dp", "ctx", None),
        P("dp", "ctx", None),
        P("dp", None, "ctx"),
        P("dp"),
        P("dp"),
        P("dp"),
    )
    return jax.shard_map(
        per_device, mesh=mesh, in_specs=in_specs, out_specs=out_specs, check_vma=False
    )
```

profile of v0, /device:TPU:2, one launch (start us, length us, event | category | flops | bytes accessed | tf_op | source)
XLA Modules:
  0.0 1079.0 jit_solution(3986648972201466773)
XLA Ops:
  11.7 44.5 %all-reduce.20 = (f32[64]{0:T(128)S(1)}, f32[64]{0:T(128)S(1)}, f32[64]{0:T(128)S(1)}) all-reduce(f32[64]{0:T(128)S(1)} %dynamic-update-slice.2, f32[64]{0:T(128)S(1)} %dynamic-update-slice.1, f32[64]{0:T(128)S(1)} %dynamic-update-slice), channel_id=1, replica_groups=mesh['ctx'=16,'dp'=16] {'dp'}, use_global_device_ids=true, to_apply=%add.18 | all-reduce | flops 192 | bytes 1536
  82.2 44.0 %all-reduce.19 = f32[1024]{0:T(1024)S(1)} all-reduce(f32[1024]{0:T(1024)S(1)} %dynamic-update-slice.3), channel_id=2, replica_groups=mesh['ctx'=16,'dp'=16] {'ctx'}, use_global_device_ids=true, to_apply=%add.19 | all-reduce | flops 1024 | bytes 8192
  137.2 3.9 fusion.167
  141.1 288.0 %all-gather.6.cloned.1.call-done = f32[1024,64,64]{2,1,0:T(8,128)} async-done(((f32[64,64,64]{2,1,0:T(8,128)}), f32[1024,64,64]{2,1,0:T(8,128)}) %all-gather.6.cloned.1.call-update) | async-done | bytes 16777232 | tf_op jit(solution)/shard_map/all_gather | solution.py:19
  429.4 40.8 %while.16 = (s32[]{:T(128)}, f32[64,64,64]{2,1,0:T(8,128)S(1)}, s32[]{:T(128)}, f32[16,64]{1,0:T(8,128)}, f32[16,64,64,64]{3,2,1,0:T(8,128)}, /*index=5*/s32[]{:T(128)}, s32[]{:T(128)}, s32[]{:T(128)}, s32[]{:T(128)}) while((s32[]{:T(128)}, f32[64,64,64]{2,1,0:T(8,128)S(1)}, s32[]{:T(128)}, f32[16,64]{1,0:T(8,128)}, ...), condition=%wide.region_9.10_spmd, body=%wide.region_8.9_spmd.sunk | while | flops 524294 | bytes 3146651 | solution.py:28
  430.1 2.0 bitcast_add_fusion.20
  438.2 2.2 bitcast_add_fusion.20
  451.9 2.0 bitcast_add_fusion.20
  454.6 2.0 bitcast_add_fusion.20
  457.3 2.0 bitcast_add_fusion.20
  462.7 2.0 bitcast_add_fusion.20
  468.1 2.0 bitcast_add_fusion.20
  470.2 312.5 %all-gather.8.cloned.1.call-done = f32[1024,64,64]{2,1,0:T(8,128)} async-done(((f32[64,64,64]{2,1,0:T(8,128)}), f32[1024,64,64]{2,1,0:T(8,128)}) %all-gather.8.cloned.1.call-update) | async-done | bytes 16777232 | tf_op jit(solution)/shard_map/all_gather | solution.py:19
  784.5 2.5 multiply_reduce_fusion.9
  792.3 2.1 multiply_reduce_fusion.22
  799.7 2.1 multiply_reduce_fusion.20
  807.2 2.1 multiply_reduce_fusion.18
  814.7 2.1 multiply_reduce_fusion.16
  822.3 2.1 multiply_reduce_fusion.14
  828.3 2.1 multiply_reduce_fusion.12
  833.1 2.1 multiply_reduce_fusion.10
  837.3 2.2 multiply_reduce_fusion.8
  860.4 2.4 copy.177
  930.4 140.3 %psum.7 = f32[3,64]{1,0:T(4,128)S(1)} all-reduce(f32[3,64]{1,0:T(4,128)S(1)} %pad_maximum_fusion), channel_id=1, replica_groups=mesh['ctx'=16,'dp'=16] {'ctx','dp'}, use_global_device_ids=true, to_apply=%region_124.126 | all-reduce | flops 192 | bytes 1536 | tf_op jit(solution)/shard_map/psum | solution.py:195
  (538 shorter events, 191.8 us)
Async XLA Ops:
  7.2 59.4 %copy-start.5 = (f32[1,64,128]{2,1,0:T(8,128)S(1)}, f32[1,64,128]{2,1,0:T(8,128)}, u32[]{:S(2)}) copy-start(f32[1,64,128]{2,1,0:T(8,128)} %param.16) | copy-start | bytes 98308
  7.2 59.3 %copy-start.19 = (bf16[1,128,512]{2,1,0:T(8,128)(2,1)S(1)}, bf16[1,128,512]{2,1,0:T(8,128)(2,1)}, u32[]{:S(2)}) copy-start(bf16[1,128,512]{2,1,0:T(8,128)(2,1)} %param.15) | copy-start | bytes 393220
  7.2 422.0 %all-gather.6.cloned.1.call-start = ((), (), s32[]{:S(2)}) async-start(), calls=%async_computation | async-start | bytes 35651584 | tf_op jit(solution)/shard_map/all_gather | solution.py:19
  70.8 711.9 %all-gather.8.cloned.1.call-start = ((), (), s32[]{:S(2)}) async-start(), calls=%async_computation.1 | async-start | bytes 35651584 | tf_op jit(solution)/shard_map/all_gather | solution.py:19
  72.5 64.6 %copy-start.2 = (bf16[1,128,4096]{1,2,0:T(8,128)(2,1)}, bf16[1,128,4096]{1,2,0:T(8,128)(2,1)S(1)}, u32[]{:S(2)}) copy-start(bf16[1,128,4096]{1,2,0:T(8,128)(2,1)S(1)} %copy.144) | copy-start | bytes 3145732
  78.5 53.1 %copy-start.53 = (f32[128,8]{0,1:T(8,128)S(1)}, f32[128,8]{0,1:T(8,128)}, u32[]{:S(2)}) copy-start(f32[128,8]{0,1:T(8,128)} %get-tuple-element.672) | copy-start | bytes 12292
  80.4 51.8 %copy-start.59 = (f32[128,8]{0,1:T(8,128)S(1)}, f32[128,8]{0,1:T(8,128)}, u32[]{:S(2)}) copy-start(f32[128,8]{0,1:T(8,128)} %get-tuple-element.677) | copy-start | bytes 12292
  80.4 52.4 %copy-start.49 = (f32[128,8]{0,1:T(8,128)S(1)}, f32[128,8]{0,1:T(8,128)}, u32[]{:S(2)}) copy-start(f32[128,8]{0,1:T(8,128)} %get-tuple-element.669) | copy-start | bytes 12292
  80.5 53.0 %copy-start.57 = (f32[128,8]{0,1:T(8,128)S(1)}, f32[128,8]{0,1:T(8,128)}, u32[]{:S(2)}) copy-start(f32[128,8]{0,1:T(8,128)} %get-tuple-element.656) | copy-start | bytes 12292
  871.8 17.3 %copy-start.69 = (f32[128,8]{0,1:T(8,128)S(1)}, f32[128,8]{0,1:T(8,128)}, u32[]{:S(2)}) copy-start(f32[128,8]{0,1:T(8,128)} %fusion.28) | copy-start | bytes 12292
  871.8 17.3 %copy-start.71 = (f32[8,1,1]{2,0,1:T(8,128)S(1)}, f32[8,1,1]{2,0,1:T(8,128)}, u32[]{:S(2)}) copy-start(f32[8,1,1]{2,0,1:T(8,128)} %get-tuple-element.704) | copy-start | bytes 100
  871.9 17.3 %copy-start.123 = (f32[8,128]{1,0:T(8,128)S(1)}, f32[8,128]{1,0:T(8,128)}, u32[]{:S(2)}) copy-start(f32[8,128]{1,0:T(8,128)} %get-tuple-element.581) | copy-start | bytes 12292
  871.9 19.8 %copy-start.61 = (f32[8,128]{1,0:T(8,128)S(1)}, f32[8,128]{1,0:T(8,128)}, u32[]{:S(2)}) copy-start(f32[8,128]{1,0:T(8,128)} %get-tuple-element.554) | copy-start | bytes 12292
  871.9 20.7 %copy-start.68 = (f32[128,8]{0,1:T(8,128)S(1)}, f32[128,8]{0,1:T(8,128)}, u32[]{:S(2)}) copy-start(f32[128,8]{0,1:T(8,128)} %fusion.29) | copy-start | bytes 12292
  871.9 20.7 %copy-start.70 = (f32[8,1,1]{2,0,1:T(8,128)S(1)}, f32[8,1,1]{2,0,1:T(8,128)}, u32[]{:S(2)}) copy-start(f32[8,1,1]{2,0,1:T(8,128)} %get-tuple-element.700) | copy-start | bytes 100
  871.9 20.7 %copy-start.121 = (f32[8,128]{1,0:T(8,128)S(1)}, f32[8,128]{1,0:T(8,128)}, u32[]{:S(2)}) copy-start(f32[8,128]{1,0:T(8,128)} %get-tuple-element.530) | copy-start | bytes 12292
  871.9 20.7 %copy-start.122 = (f32[8,128]{1,0:T(8,128)S(1)}, f32[8,128]{1,0:T(8,128)}, u32[]{:S(2)}) copy-start(f32[8,128]{1,0:T(8,128)} %get-tuple-element.531) | copy-start | bytes 12292
  898.7 17.9 %copy-start.76 = (f32[8,128]{1,0:T(8,128)S(1)}, f32[8,128]{1,0:T(8,128)}, u32[]{:S(2)}) copy-start(f32[8,128]{1,0:T(8,128)} %get-tuple-element.714) | copy-start | bytes 12292
  898.7 19.2 %copy-start.74 = (f32[8,128]{1,0:T(8,128)S(1)}, f32[8,128]{1,0:T(8,128)}, u32[]{:S(2)}) copy-start(f32[8,128]{1,0:T(8,128)} %get-tuple-element.718) | copy-start | bytes 12292
  901.6 19.4 %copy-start.3 = (bf16[1,128,4096]{1,2,0:T(8,128)(2,1)S(1)}, bf16[1,128,4096]{1,2,0:T(8,128)(2,1)}, u32[]{:S(2)}) copy-start(bf16[1,128,4096]{1,2,0:T(8,128)(2,1)} %copy-done.2) | copy-start | bytes 3145732
  901.7 19.4 %copy-start.14 = (f32[128,8,64]{0,2,1:T(8,128)S(1)}, f32[128,8,64]{0,2,1:T(8,128)}, u32[]{:S(2)}) copy-start(f32[128,8,64]{0,2,1:T(8,128)} %get-tuple-element.763) | copy-start | bytes 786436
  901.7 19.4 %copy-start.15 = (f32[128,8,64]{0,2,1:T(8,128)S(1)}, f32[128,8,64]{0,2,1:T(8,128)}, u32[]{:S(2)}) copy-start(f32[128,8,64]{0,2,1:T(8,128)} %get-tuple-element.765) | copy-start | bytes 786436
  901.7 19.4 %copy-start.16 = (f32[128,8,64]{0,2,1:T(8,128)S(1)}, f32[128,8,64]{0,2,1:T(8,128)}, u32[]{:S(2)}) copy-start(f32[128,8,64]{0,2,1:T(8,128)} %get-tuple-element.767) | copy-start | bytes 786436
  901.7 19.4 %copy-start.17 = (f32[128,8,64]{0,2,1:T(8,128)S(1)}, f32[128,8,64]{0,2,1:T(8,128)}, u32[]{:S(2)}) copy-start(f32[128,8,64]{0,2,1:T(8,128)} %get-tuple-element.769) | copy-start | bytes 786436
  (125 other events, 870.6 us)
Sparse Core Ops, SparseCore 0:
  70.9 358.1 all-gather.5
  430.9 351.7 all-gather.7
where the time goes:
time: 1090 us; the launch traced here: 1080 us
  waiting for transfers between devices  601 us (55%)
  blocking collectives  229 us (21%)
  matrix products  99.1 us (9%)
  other arithmetic  90 us (8%)
  local copies, waits for them, and re-layouts  42.4 us (4%)
  between operations  17.4 us (2%)
    all_gather x2, waiting for transfers between devices, carried_in(): gathered = jax.tree.map(lambda a: lax.all_gather(a, axis), part)  601 us
    psum x1, blocking collectives, per_device(): summed = lax.psum(head_stats, ('ctx', 'dp'))  140 us
    unnamed x2, blocking collectives  88.5 us
    add x15, other arithmetic, chain_pair(): later[0][:, None, None] * earlier[1] + later[1]  29.9 us
    dot_general x16, matrix products, group_scan(): jnp.einsum('hckn,ckhp->chpn', weighted_b, scaled, precision=highest)  28.9 us
    another operation x24, other arithmetic, group_scan(): cumulative = jnp.cumsum(log_decay.reshape(num_heads, blocks, SPAN), axis=2)  24 us
    dot_general x24, matrix products, group_scan(): scores = jnp.einsum('cqn,ckn->cqk', c_blocks, b_blocks, precision=highest)  22.9 us
    dot_general x16, matrix products, group_scan(): jnp.einsum('hcqk,ckhp->cqhp', weights * scores[None], scaled, precision=h...  22 us
  transfers between devices with their start and end apart: 2, of which 2 were waited for; matrix products, arithmetic and copies ran while one was open for 6% of the time, Pallas kernels for 0%

commit v1 on v0

v1 whole, which is shorter than its diff:
```python
import jax
import jax.numpy as jnp
from jax import lax
from jax.sharding import PartitionSpec as P

P_SIZE = 64
N = 64
G = 8


highest = lax.Precision.HIGHEST


def slab_scan(x, b, c, raw, bias, alog, skip, state_in):
    tokens, num_heads, width = x.shape
    group_heads = num_heads // G
    dt_value = jax.nn.softplus(raw + bias[:, None])
    log_decay = dt_value * (-jnp.exp(alog))[:, None]
    cumulative = jnp.cumsum(log_decay, axis=1)
    scaled = (x * dt_value.T[:, :, None]).reshape(tokens, G, group_heads, width)
    scores = jnp.einsum("qgn,kgn->gqk", c, b, precision=highest)
    offsets = jnp.arange(tokens)
    causal = offsets[:, None] >= offsets[None, :]
    spread = cumulative[:, :, None] - cumulative[:, None, :]
    weights = jnp.where(causal, jnp.exp(jnp.where(causal, spread, 0.0)), 0.0)
    mixed = weights.reshape(G, group_heads, tokens, tokens) * scores[:, None]
    local_part = jnp.einsum("gjqk,kgjp->qgjp", mixed, scaled, precision=highest)
    tail_decay = jnp.exp(cumulative[:, -1:] - cumulative)
    weighted_b = b[:, :, None, :] * tail_decay.T.reshape(tokens, G, group_heads)[:, :, :, None]
    block_state = jnp.einsum("kgjn,kgjp->gjpn", weighted_b, scaled, precision=highest)
    block_state = block_state.reshape(num_heads, width, N)
    state_out = jnp.exp(cumulative[:, -1])[:, None, None] * state_in + block_state
    entering = state_in.reshape(G, group_heads, width, N)
    cross_part = jnp.einsum("qgn,gjpn->qgjp", c, entering, precision=highest)
    cross_part = cross_part * jnp.exp(cumulative).T.reshape(tokens, G, group_heads)[:, :, :, None]
    result = (local_part + cross_part).reshape(tokens, num_heads, width)
    result = result + skip[None, :, None] * x
    return (result, state_out)


def slab_terms(x, b, c, raw, bias, alog, grad):
    tokens, num_heads, width = x.shape
    group_heads = num_heads // G
    dt_value = jax.nn.softplus(raw + bias[:, None])
    log_decay = dt_value * (-jnp.exp(alog))[:, None]
    cumulative = jnp.cumsum(log_decay, axis=1)
    total = cumulative[:, -1]
    tail_decay = jnp.exp(total[:, None] - cumulative)
    carried = (x * (dt_value * tail_decay).T[:, :, None]).reshape(tokens, G, group_heads, width)
    local_state = jnp.einsum("tgn,tgjp->gjpn", b, carried, precision=highest)
    weighted_grad = (grad * jnp.exp(cumulative).T[:, :, None]).reshape(tokens, G, group_heads, width)
    local_source = jnp.einsum("tgn,tgjp->gjpn", c, weighted_grad, precision=highest)
    return (
        total,
        local_state.reshape(num_heads, width, N),
        local_source.reshape(num_heads, width, N),
    )


def carry_across(total, local_state, local_source):
    count = lax.axis_size("ctx")
    num_heads = total.shape[0]
    share = num_heads // count
    lanes = local_state.shape[2]
    payload = jnp.concatenate(
        [local_state, local_source, jnp.broadcast_to(total[:, None, None], (num_heads, 1, lanes))],
        axis=1,
    )
    got = lax.all_to_all(payload, "ctx", 0, 0, tiled=True)
    got = got.reshape(count, share, got.shape[1], lanes)
    width = local_state.shape[1]
    states = got[:, :, :width].reshape(count, share, width * lanes)
    sources = got[:, :, width : 2 * width].reshape(count, share, width * lanes)
    totals = got[:, :, 2 * width, 0]
    slab = jnp.arange(count)
    between = (slab[None, :, None] < slab[None, None, :]) & (slab[None, None, :] < slab[:, None, None])
    exponent = jnp.einsum("jim,mh->jih", between.astype(jnp.float32), totals, precision=highest)
    before = slab[None, :] < slab[:, None]
    chain = jnp.where(before[:, :, None], jnp.exp(jnp.where(before[:, :, None], exponent, 0.0)), 0.0)
    entering = jnp.einsum("jih,ihx->jhx", chain, states, precision=highest)
    leaving = jnp.einsum("jkh,jhx->khx", chain, sources, precision=highest)
    back = jnp.concatenate(
        [entering.reshape(count * share, width, lanes), leaving.reshape(count * share, width, lanes)],
        axis=1,
    )
    mine = lax.all_to_all(back, "ctx", 0, 0, tiled=True)
    return mine[:, :width], mine[:, width:]


def per_device(inputs, b_proj, c_proj, dt_raw, a_log, dt_bias, d_skip, grad_out):
    params = lax.all_gather(jnp.stack([a_log, dt_bias, d_skip]), "dp", axis=1, tiled=True)
    alog_all, bias_all, skip_all = params[0], params[1], params[2]
    tokens = inputs.shape[1]
    num_heads = alog_all.shape[0]
    x = inputs[0].astype(jnp.float32).reshape(tokens, num_heads, P_SIZE)
    grad = grad_out[0].astype(jnp.float32).reshape(tokens, num_heads, P_SIZE)
    b = b_proj[0].astype(jnp.float32).reshape(tokens, G, N)
    c = c_proj[0].astype(jnp.float32).reshape(tokens, G, N)
    raw = dt_raw[0]
    total, local_state, local_source = slab_terms(x, b, c, raw, bias_all, alog_all, grad)
    entering, leaving = carry_across(total, local_state, local_source)
    _, pullback = jax.vjp(slab_scan, x, b, c, raw, bias_all, alog_all, skip_all, entering)
    gx, gb, gc, graw, gbias, galog, gskip, _ = pullback((grad, leaving))
    grad_inputs = gx.reshape(tokens, num_heads * P_SIZE).astype(jnp.bfloat16)[None]
    grad_b = gb.reshape(tokens, G * N).astype(jnp.bfloat16)[None]
    grad_c = gc.reshape(tokens, G * N).astype(jnp.bfloat16)[None]
    grad_dt = graw[None]
    head_stats = jnp.stack([galog, gbias, gskip], axis=0)
    share_size = num_heads // lax.axis_size("dp")
    summed = lax.psum(head_stats, ("ctx", "dp"))
    own_totals = lax.dynamic_slice_in_dim(summed, lax.axis_index("dp") * share_size, share_size, 1)
    return (grad_inputs, grad_b, grad_c, grad_dt, own_totals[0], own_totals[1], own_totals[2])


def solution(mesh):
    in_specs = (
        P("dp", "ctx", None),
        P("dp", "ctx", None),
        P("dp", "ctx", None),
        P("dp", None, "ctx"),
        P("dp"),
        P("dp"),
        P("dp"),
        P("dp", "ctx", None),
    )
    out_specs = (
        P("dp", "ctx", None),
        P("dp", "ctx", None),
        P("dp", "ctx", None),
        P("dp", None, "ctx"),
        P("dp"),
        P("dp"),
        P("dp"),
    )
    return jax.shard_map(
        per_device, mesh=mesh, in_specs=in_specs, out_specs=out_specs, check_vma=False
    )
```

time: 1090 us -> 348 us (0.32)
  waiting for transfers between devices: 601 us -> 108 us
  blocking collectives: 229 us -> 111 us
  other arithmetic: 90 us -> 18.2 us
  matrix products: 99.1 us -> 43.3 us
  starting transfers between devices: 0.08 us -> 24.9 us
  between operations: 17.4 us -> 1.11 us
    all_gather x2 -> x0, waiting for transfers between devices: 601 us -> none  [carried_in(): gathered = jax.tree.map(lambda a: lax.all_gather(a, axis), part)]
    all_to_all x0 -> x2, waiting for transfers between devices: none -> 108 us  [the longest x1 80.2 us: carry_across(): got = lax.all_to_all(payload, 'ctx', 0, 0, tiled=True)]
    unnamed x2 -> x0, blocking collectives: 88.5 us -> none
    psum x1, blocking collectives: 140 us -> 79.8 us  [per_device(): summed = lax.psum(head_stats, ('ctx', 'dp'))]
    dot_general x88 -> x14, matrix products: 99.1 us -> 43.3 us  [the longest x2 13.3 us: slab_scan(): local_part = jnp.einsum('gjqk,kgjp->qgjp', mixed, scaled, precision=highest)]
    all_gather x0 -> x1, blocking collectives: none -> 31.1 us  [per_device(): lax.all_gather(jnp.stack([a_log, dt_bias, d_skip]), 'dp', axis=1, tiled=T...]
    add x15 -> x1, other arithmetic: 29.9 us -> 0.01 us  [slab_terms(): dt_value = jax.nn.softplus(raw + bias[:, None])]
    all_to_all x0 -> x2, starting transfers between devices: none -> 24.9 us  [the longest x1 18.9 us: carry_across(): mine = lax.all_to_all(back, 'ctx', 0, 0, tiled=True)]
  transfers between devices with their start and end apart: 2 -> 2, of which waited for: 2 -> 2; matrix products, arithmetic and copies ran while one was open for 6% -> 4% of each run, Pallas kernels for 0% -> 0%
where the time goes in v1:
time: 348 us; the launch traced here: 345 us
  blocking collectives  111 us (32%)
  waiting for transfers between devices  108 us (31%)
  matrix products  43.3 us (12%)
  local copies, waits for them, and re-layouts  38.9 us (11%)
  starting transfers between devices  24.9 us (7%)
  other arithmetic  18.2 us (5%)
    all_to_all x1, waiting for transfers between devices, carry_across(): got = lax.all_to_all(payload, 'ctx', 0, 0, tiled=True)  80.2 us
    psum x1, blocking collectives, per_device(): summed = lax.psum(head_stats, ('ctx', 'dp'))  79.8 us
    all_gather x1, blocking collectives, per_device(): lax.all_gather(jnp.stack([a_log, dt_bias, d_skip]), 'dp', axis=1, tiled=T...  31.1 us
    all_to_all x1, waiting for transfers between devices, carry_across(): mine = lax.all_to_all(back, 'ctx', 0, 0, tiled=True)  27.6 us
    all_to_all x1, starting transfers between devices, carry_across(): mine = lax.all_to_all(back, 'ctx', 0, 0, tiled=True)  18.9 us
    dot_general x2, matrix products, slab_scan(): local_part = jnp.einsum('gjqk,kgjp->qgjp', mixed, scaled, precision=highest)  13.3 us
    dot_general x2, matrix products, slab_scan(): jnp.einsum('kgjn,kgjp->gjpn', weighted_b, scaled, precision=highest)  10.5 us
    unnamed x51, local copies, waits for them, and re-layouts  8.07 us
  transfers between devices with their start and end apart: 2, of which 2 were waited for; matrix products, arithmetic and copies ran while one was open for 4% of the time, Pallas kernels for 0%

profile of v1, /device:TPU:2, one launch (start us, length us, event | category | flops | bytes accessed | tf_op | source)
XLA Modules:
  0.0 345.0 jit_solution(9068073911150541548)
XLA Ops:
  1.5 31.1 %all-gather = f32[16,4,3]{2,1,0:T(4,128)S(1)} all-gather(f32[1,4,3]{2,1,0:T(4,128)S(1)} %bitcast.241), channel_id=1, replica_groups=mesh['ctx'=16,'dp'=16] {'dp'}, dimensions={0}, use_global_device_ids=true | all-gather | bytes 816 | tf_op jit(solution)/shard_map/all_gather | solution.py:91
  39.7 3.9 %fusion.9 = f32[8,8,64,64]{2,3,1,0:T(8,128)S(1)} fusion(bf16[128,8,64,1]{0,2,3,1:T(8,128)(2,1)S(1)} %bitcast.214, bf16[128,8,8,64]{0,3,2,1:T(8,128)(2,1)S(1)} %bitcast.198, f32[128,8,8]{0,2,1:T(8,128)} %bitcast.224), kind=kOutput, calls=%fused_computation.19 | convolution fusion | flops 403701760 | bytes 2260992 | tf_op jit(solution)/shard_map/tgn,tgjp->gjpn/dot_general | solution.py:52
  43.6 3.1 fusion.26
  47.0 3.2 pad_maximum_fusion
  50.2 6.0 %all-to-all-start = ((f32[64,129,64]{1,2,0:T(8,128)}), f32[64,129,64]{1,2,0:T(8,128)}, u32[]{:S(2)}, u32[]{:S(2)}) async-start(f32[64,129,64]{1,2,0:T(8,128)} %pad_maximum_fusion), calls=%async_computation | async-start | bytes 8388608 | tf_op jit(solution)/shard_map/all_to_all | solution.py:69
  56.2 80.2 %all-to-all-done = f32[64,129,64]{1,2,0:T(8,128)} async-done(((f32[64,129,64]{1,2,0:T(8,128)}), f32[64,129,64]{1,2,0:T(8,128)}, u32[]{:S(2)}, u32[]{:S(2)}) %all-to-all-start) | async-done | bytes 2113568 | tf_op jit(solution)/shard_map/all_to_all | solution.py:69
  137.3 4.9 %fusion.68 = (f32[16,4,64,64]{2,3,1,0:T(8,128)}, f32[16,4,64,64]{2,3,1,0:T(8,128)}) fusion(f32[16,4,129,64]{2,3,1,0:T(8,128)} %bitcast.26), kind=kLoop, calls=%fused_computation.110 | loop fusion | bytes 4194304 | tf_op jit(solution)/shard_map/slice | solution.py:72
  143.6 3.0 copy.200
  146.6 2.1 reshape.270
  151.2 2.4 reshape.271
  153.6 3.0 copy.204
  161.1 2.3 reshape.273
  163.4 4.7 %pad_maximum_fusion.1 = f32[64,128,64]{2,1,0:T(8,128)} fusion(f32[64,64,64]{2,1,0:T(8,128)} %reshape.273, f32[64,64,64]{2,1,0:T(8,128)} %reshape.271), kind=kLoop, calls=%fused_computation.3 | loop fusion | flops 524288 | bytes 4194304 | tf_op jit(solution)/shard_map/concatenate | solution.py:82
  168.1 3.8 %copy.207 = f32[64,128,64]{1,2,0:T(8,128)} copy(f32[64,128,64]{2,1,0:T(8,128)} %pad_maximum_fusion.1) | data formatting | bytes 4194304 | tf_op jit(solution)/shard_map/concatenate | solution.py:82
  172.0 18.9 %all-to-all-start.1 = ((f32[64,128,64]{1,2,0:T(8,128)}), f32[64,128,64]{1,2,0:T(8,128)}, u32[]{:S(2)}, u32[]{:S(2)}) async-start(f32[64,128,64]{1,2,0:T(8,128)} %copy.207), calls=%async_computation.1 | async-start | bytes 4194304 | tf_op jit(solution)/shard_map/all_to_all | solution.py:86
  191.4 7.1 %fusion.11 = (f32[8,8,128]{2,1,0:T(8,128)S(1)}, f32[8,8,128]{2,1,0:T(8,128)}, f32[8,128,128]{1,2,0:T(8,128)}) fusion(f32[8,128,128]{1,2,0:T(8,128)S(1)} %fusion.72, f32[8,8,128]{2,1,0:T(8,128)S(1)} %bitcast.235, pred[128,128]{0,1:T(8,128)(4,1)S(1)} %iota_compare_fusion, bf16[8,8,64,128]{3,2,1,0:T(8,128)(2,1)S(1)} %bitcast.199, ...), kind=kOutput, calls=%fused_computation.21 | convolution fusion | flops 817741824 | bytes 3293184 | tf_op jit(solution)/shard_map/transpose(jvp(gjqk,kgjp->qgjp))/dot_general | solution.py:27
  199.6 6.2 %fusion.4 = f32[8,8,128,64]{2,3,1,0:T(8,128)} fusion(bf16[8,8,64,128]{3,2,1,0:T(8,128)(2,1)S(1)} %bitcast.200, f32[8,128,128]{1,2,0:T(8,128)S(1)} %fusion.72, f32[8,8,128]{2,1,0:T(8,128)S(1)} %bitcast.236, pred[128,128]{0,1:T(8,128)(4,1)S(1)} %iota_compare_fusion), kind=kOutput, calls=%fused_computation.10 | convolution fusion | flops 809500672 | bytes 3719168 | tf_op jit(solution)/shard_map/transpose(jvp(gjqk,kgjp->qgjp))/dot_general | solution.py:27
  205.7 27.6 %all-to-all-done.1 = f32[64,128,64]{1,2,0:T(8,128)} async-done(((f32[64,128,64]{1,2,0:T(8,128)}), f32[64,128,64]{1,2,0:T(8,128)}, u32[]{:S(2)}, u32[]{:S(2)}) %all-to-all-start.1) | async-done | bytes 2097184 | tf_op jit(solution)/shard_map/all_to_all | solution.py:86
  233.3 3.7 %multiply_reduce_fusion = (f32[64]{0:T(128)S(1)}, f32[64,64,64]{1,2,0:T(8,128)S(1)}, f32[64,64,64]{1,2,0:T(8,128)S(1)}) fusion(f32[64,128,64]{1,2,0:T(8,128)} %all-to-all-done.1), kind=kLoop, calls=%fused_computation.33 | loop fusion | flops 524224 | bytes 4194560 | tf_op jit(solution)/shard_map/transpose(jvp())/reduce_sum | solution.py:32
  238.8 2.9 fusion.36
  241.8 3.2 fusion.19
  246.8 7.3 %multiply_reduce_fusion.1 = (f32[128,8,8]{0,2,1:T(8,128)S(1)}, f32[128,8,8,64]{0,3,2,1:T(8,128)}) fusion(f32[8,8,128,64]{2,3,1,0:T(8,128)} %fusion.4, f32[8,8,64,64]{2,3,1,0:T(8,128)} %bitcast.208, f32[128,8,8]{0,2,1:T(8,128)S(1)} %bitcast.227, f32[128,8,64]{0,2,1:T(8,128)S(1)} %convert_element_type.70, bf16[128,8,8,64]{0,3,2,1:T(8,128)(2,1)S(1)} %bitcast.206), kind=kOutput, calls=%fused_computation.34 | convolution fusion | flops 405266432 | bytes 6619136 | tf_op jit(solution)/shard_map/transpose(jvp(kgjn,kgjp->gjpn))/dot_general | solution.py:30
  255.1 2.5 fusion.16
  257.8 79.8 %psum.7 = f32[3,64]{1,0:T(4,128)S(1)} all-reduce(f32[3,64]{1,0:T(4,128)S(1)} %pad_maximum_fusion.2), channel_id=1, replica_groups=mesh['ctx'=16,'dp'=16] {'ctx','dp'}, use_global_device_ids=true, to_apply=%region_15.16 | all-reduce | flops 192 | bytes 1536 | tf_op jit(solution)/shard_map/psum | solution.py:110
  (101 shorter events, 31.0 us)
Async XLA Ops:
  0.6 36.5 %copy-start.11 = (bf16[1,128,512]{2,1,0:T(8,128)(2,1)S(1)}, bf16[1,128,512]{2,1,0:T(8,128)(2,1)}, u32[]{:S(2)}) copy-start(bf16[1,128,512]{2,1,0:T(8,128)(2,1)} %param.10) | copy-start | bytes 393220
  0.6 37.4 %copy-start.1 = (bf16[1,128,4096]{2,1,0:T(8,128)(2,1)S(1)}, bf16[1,128,4096]{2,1,0:T(8,128)(2,1)}, u32[]{:S(2)}) copy-start(bf16[1,128,4096]{2,1,0:T(8,128)(2,1)} %param.8) | copy-start | bytes 3145732
  32.7 0.9 copy-start.16
  32.7 0.9 copy-start.18
  32.7 2.8 copy-start.14
  34.0 1.5 copy-start.9
  34.1 12.6 %copy-start.12 = (f32[64]{0:T(128)}, f32[64]{0:T(128)S(1)}, u32[]{:S(2)}) copy-start(f32[64]{0:T(128)S(1)} %slice_bitcast_fusion.5) | copy-start | bytes 772
  38.7 4.9 %copy-start.8 = (f32[128,64]{0,1:T(8,128)S(1)}, f32[128,64]{0,1:T(8,128)}, u32[]{:S(2)}) copy-start(f32[128,64]{0,1:T(8,128)} %copy.194) | copy-start | bytes 98308
  50.2 86.2 %all-to-all-start = ((f32[64,129,64]{1,2,0:T(8,128)}), f32[64,129,64]{1,2,0:T(8,128)}, u32[]{:S(2)}, u32[]{:S(2)}) async-start(f32[64,129,64]{1,2,0:T(8,128)} %pad_maximum_fusion), calls=%async_computation | async-start | bytes 8388608 | tf_op jit(solution)/shard_map/all_to_all | solution.py:69
  172.0 19.0 %copy-start.6 = (f32[128,64]{1,0:T(8,128)S(1)}, f32[128,64]{1,0:T(8,128)}, u32[]{:S(2)}) copy-start(f32[128,64]{1,0:T(8,128)} %get-tuple-element.71) | copy-start | bytes 98308
  172.0 19.0 %copy-start.5 = (f32[128,64]{1,0:T(8,128)S(1)}, f32[128,64]{1,0:T(8,128)}, u32[]{:S(2)}) copy-start(f32[128,64]{1,0:T(8,128)} %get-tuple-element.73) | copy-start | bytes 98308
  172.0 19.5 %copy-start.10 = (f32[64,128]{1,0:T(8,128)S(1)}, f32[64,128]{1,0:T(8,128)}, u32[]{:S(2)}) copy-start(f32[64,128]{1,0:T(8,128)} %copy-done.9) | copy-start | bytes 98308
  172.0 61.3 %all-to-all-start.1 = ((f32[64,128,64]{1,2,0:T(8,128)}), f32[64,128,64]{1,2,0:T(8,128)}, u32[]{:S(2)}, u32[]{:S(2)}) async-start(f32[64,128,64]{1,2,0:T(8,128)} %copy.207), calls=%async_computation.1 | async-start | bytes 4194304 | tf_op jit(solution)/shard_map/all_to_all | solution.py:86
  191.0 50.8 %copy-start.3 = (f32[128,64]{0,1:T(8,128)}, f32[128,64]{0,1:T(8,128)S(1)}, u32[]{:S(2)}) copy-start(f32[128,64]{0,1:T(8,128)S(1)} %copy.212) | copy-start | bytes 98308
  237.0 4.8 %copy-start = (f32[64,64,64]{1,2,0:T(8,128)}, f32[64,64,64]{1,2,0:T(8,128)S(1)}, u32[]{:S(2)}) copy-start(f32[64,64,64]{1,2,0:T(8,128)S(1)} %get-tuple-element.67) | copy-start | bytes 3145732
  237.0 1.8 copy-start.2
  241.8 3.3 copy-start.13
  246.7 7.4 %copy-start.15 = (f32[64]{0:T(128)S(1)}, f32[64]{0:T(128)}, u32[]{:S(2)}) copy-start(f32[64]{0:T(128)} %copy-done.14) | copy-start | bytes 772
  246.8 7.4 %copy-start.19 = (f32[64]{0:T(128)S(1)}, f32[64]{0:T(128)}, u32[]{:S(2)}) copy-start(f32[64]{0:T(128)} %copy-done.18) | copy-start | bytes 772
  246.8 8.1 %copy-start.17 = (f32[64,3]{0,1:T(4,128)S(1)}, f32[64,3]{0,1:T(4,128)}, u32[]{:S(2)}) copy-start(f32[64,3]{0,1:T(4,128)} %copy-done.16) | copy-start | bytes 2308
  246.8 8.3 %copy-start.4 = (f32[128,64]{0,1:T(8,128)S(1)}, f32[128,64]{0,1:T(8,128)}, u32[]{:S(2)}) copy-start(f32[128,64]{0,1:T(8,128)} %copy-done.3) | copy-start | bytes 98308
  339.6 4.6 %copy-start.7 = (f32[64,128]{0,1:T(8,128)S(1)}, f32[64,128]{0,1:T(8,128)}, u32[]{:S(2)}) copy-start(f32[64,128]{0,1:T(8,128)} %get-tuple-element.62) | copy-start | bytes 98308
